TPU v7x, 512 devices: a whole 4x4x16 slice. The times are simulated.
512 devices in a mesh: path: 32 (over x, y, core), tensor: 16 (over z).
Axes of the slice: x: 4, y: 4, z: 16, core: 2. Of those that a mesh axis runs over, the one named last changes fastest.
Arguments:
- hidden_in: bfloat16 [12288, 2048], P(('path', 'tensor')), may hold values from -120 to 120
- teacher: bfloat16 [12288, 2048], P('path'), may hold values from -3 to 3
- params: bfloat16 [3, 3, 7168, 2048], P(None, None, ('tensor', 'path')), may hold values from -4 to 4
- momentum: float32 [3, 3, 7168, 2048], P(None, None, ('tensor', 'path')), may hold values from -3 to 3
- path_alive: int32 [32], replicated, may hold values from 0 to 1, as said below
- path_module: int32 [32], replicated, may hold values from 0 to 2, as said below
Outputs:
- new_params: bfloat16 [3, 3, 7168, 2048], P(None, None, ('tensor', 'path'))
- new_momentum: float32 [3, 3, 7168, 2048], P(None, None, ('tensor', 'path'))
Inputs may be any that keep to these rules, and one draw needn't show every extreme that they name: `path_alive`: at least one path is dead. `path_module`: every one of the 3 modules is used by at least one path whose path_alive entry is 1.
All inputs are finite; a program needn't handle non-finite values.
Results may differ from a plain program's by a relative error of at most 0.0047.
Values may be sent and summed in bfloat16 or wider, within the bound.
No kernel may reach another device: no remote copies, remote signals or barrier semaphores. Data moves between devices by JAX's collectives and lax.ppermute only.
A program may use at most 64 MiB of HBM per device.

v0:
```python
import math
import jax
import jax.numpy as jnp
from jax import lax
from jax.sharding import PartitionSpec as P

D = 2048
FW = 7168


def per_device(hidden_in, teacher, params, momentum, path_alive, path_module):
    module_count = params.shape[0]
    block_rows = params.shape[2]
    width = params.shape[3]
    path_count = path_alive.shape[0]
    contract_last = (((1,), (1,)), ((), ()))
    contract_first = (((0,), (0,)), ((), ()))
    picked = jnp.transpose(jnp.take(params, path_module, axis=0, mode="clip"), (1, 2, 0, 3))
    rows = lax.all_to_all(picked, "path", split_axis=2, concat_axis=2, tiled=True)
    local_rows = path_count * block_rows
    rows = rows.reshape(3, local_rows, width)
    gate_rows, up_rows, down_rows = (rows[0], rows[1], rows[2])
    own = hidden_in.astype(jnp.float32)
    mean_sq = jnp.mean(jnp.square(own), axis=1, keepdims=True)
    own_normed = (own * lax.rsqrt(mean_sq + 1e-05)).astype(jnp.bfloat16)
    normed = lax.all_gather(own_normed, "tensor", axis=0, tiled=True)
    gate_pre = lax.dot_general(
        normed, gate_rows, contract_last, preferred_element_type=jnp.float32
    ) / math.sqrt(D)
    up_proj = lax.dot_general(
        normed, up_rows, contract_last, preferred_element_type=jnp.float32
    ) / math.sqrt(D)
    sigmoid_gate = jax.nn.sigmoid(gate_pre)
    activated = gate_pre * sigmoid_gate
    hidden = (activated * up_proj).astype(jnp.bfloat16)
    partial_out = jnp.dot(hidden, down_rows, preferred_element_type=jnp.float32) / math.sqrt(FW)
    output = lax.psum(partial_out, "tensor")
    cotangent = (4.0 * (output - teacher.astype(jnp.float32))).astype(jnp.bfloat16)
    piece_shape = (block_rows, path_count, width)

    def send_back(delta):
        return lax.all_to_all(
            delta.reshape(piece_shape), "path", split_axis=1, concat_axis=1, tiled=True
        )

    down_delta = (
        lax.dot_general(hidden, cotangent, contract_first, preferred_element_type=jnp.float32)
        / math.sqrt(FW)
    ).astype(jnp.bfloat16)
    down_got = send_back(down_delta)
    hidden_grad = lax.dot_general(
        cotangent, down_rows, contract_last, preferred_element_type=jnp.float32
    ) / math.sqrt(FW)
    gate_grad = (
        hidden_grad * up_proj * sigmoid_gate * (1.0 + gate_pre * (1.0 - sigmoid_gate))
    ).astype(jnp.bfloat16)
    up_grad = (hidden_grad * activated).astype(jnp.bfloat16)
    gate_delta = (
        lax.dot_general(gate_grad, normed, contract_first, preferred_element_type=jnp.float32)
        / math.sqrt(D)
    ).astype(jnp.bfloat16)
    gate_got = send_back(gate_delta)
    up_delta = (
        lax.dot_general(up_grad, normed, contract_first, preferred_element_type=jnp.float32)
        / math.sqrt(D)
    ).astype(jnp.bfloat16)
    up_got = send_back(up_delta)
    member = (path_module[:, None] == jnp.arange(module_count, dtype=jnp.int32)[None, :]).astype(
        jnp.int32
    ) * path_alive[:, None]
    counts = jnp.sum(member, axis=0).astype(jnp.float32)
    new_momentum = []
    new_params = []
    weighting = member.astype(jnp.bfloat16)
    for j, got in enumerate((gate_got, up_got, down_got)):
        got, weighting_j, momentum_j, params_j = lax.optimization_barrier(
            (got, weighting, momentum[:, j], params[:, j])
        )
        summed = lax.dot_general(
            weighting_j, got, (((0,), (1,)), ((), ())), preferred_element_type=jnp.float32
        )
        mean_delta = summed / counts[:, None, None]
        momentum_j = 0.9 * momentum_j + mean_delta
        params_j = (params_j.astype(jnp.float32) - 0.7 * (mean_delta + 0.9 * momentum_j)).astype(
            jnp.bfloat16
        )
        new_momentum.append(momentum_j)
        new_params.append(params_j)
    new_momentum = jnp.stack(new_momentum, axis=1)
    new_params = jnp.stack(new_params, axis=1)
    return (new_params, new_momentum)


def solution(mesh):
    return jax.shard_map(
        per_device,
        mesh=mesh,
        in_specs=(
            P(("path", "tensor"), None),
            P("path", None),
            P(None, None, ("tensor", "path"), None),
            P(None, None, ("tensor", "path"), None),
            P(),
            P(),
        ),
        out_specs=(
            P(None, None, ("tensor", "path"), None),
            P(None, None, ("tensor", "path"), None),
        ),
        check_vma=False,
    )
```

profile of v0, /device:TPU:1, one launch (start us, length us, event | category | flops | bytes accessed | tf_op | source)
XLA Modules:
  0.0 409.1 jit_solution(1168579440316608955)
XLA Ops:
  7.2 0.7 pad_clamp_fusion
  7.8 4.6 %gather_fusion = bf16[32,3,14,2048]{3,2,1,0:T(8,128)(2,1)} fusion(bf16[3,3,14,2048]{3,2,1,0:T(8,128)(2,1)} %param.8, s32[1024]{0:T(1024)S(1)} %pad_clamp_fusion), kind=kCustom, calls=%fused_computation | custom fusion | bytes 11010176 | tf_op jit(solution)/shard_map/jit(_take)/gather | solution.py:18
  12.5 11.5 %all-to-all-start = ((bf16[3,14,32,2048]{3,1,0,2:T(8,128)(2,1)}), bf16[3,14,32,2048]{3,1,0,2:T(8,128)(2,1)}, u32[]{:S(2)}, u32[]{:S(2)}) async-start(bf16[3,14,32,2048]{3,1,0,2:T(8,128)(2,1)} %bitcast.60), calls=%async_computation | async-start | bytes 12582912 | tf_op jit(solution)/shard_map/all_to_all | solution.py:19
  23.9 0.0 all-gather.2.cloned.1.call-start
  24.0 0.1 fusion.11
  24.1 0.7 fusion.12
  24.9 0.0 all-gather.2.cloned.1.call-update
  24.9 0.0 all-reduce.2.cloned.1.call-start
  24.9 76.3 %all-to-all-done = bf16[3,14,32,2048]{3,1,0,2:T(8,128)(2,1)} async-done(((bf16[3,14,32,2048]{3,1,0,2:T(8,128)(2,1)}), bf16[3,14,32,2048]{3,1,0,2:T(8,128)(2,1)}, u32[]{:S(2)}, u32[]{:S(2)}) %all-to-all-start) | async-done | bytes 5505056 | tf_op jit(solution)/shard_map/all_to_all | solution.py:19
  101.3 4.0 fusion.19
  105.3 2.2 copy.35
  107.5 2.3 copy.36
  109.8 1.0 copy.37
  110.8 0.0 all-gather.2.cloned.1.call-done
  110.8 3.3 convolution_multiply_fusion.3
  114.1 2.0 multiply_convert_fusion.6
  116.1 0.7 copy-done.3
  116.8 2.7 convolution_multiply_fusion
  119.6 149.8 %all-reduce.2.cloned.1.call-done = f32[384,2048]{1,0:T(8,128)} async-done(((f32[384,2048]{1,0:T(8,128)}), f32[384,2048]{1,0:T(8,128)}) %all-reduce.2.cloned.1.call-update) | async-done | bytes 3145744 | tf_op jit(solution)/shard_map/psum | solution.py:37
  269.4 3.2 convolution_multiply_fusion.1
  272.6 1.1 multiply_convert_fusion.1
  273.8 2.3 copy.42
  276.2 17.1 %all-to-all-start.2 = ((bf16[14,32,2048]{2,0,1:T(8,128)(2,1)}), bf16[14,32,2048]{2,0,1:T(8,128)(2,1)}, u32[]{:S(2)}, u32[]{:S(2)}) async-start(bf16[14,32,2048]{2,0,1:T(8,128)(2,1)} %copy.42), calls=%async_computation.2 | async-start | bytes 4194304 | tf_op jit(solution)/shard_map/all_to_all | solution.py:42
  293.3 2.4 multiply_convert_fusion.2
  295.6 2.4 copy.38
  298.1 23.6 %all-to-all-done.2 = bf16[14,32,2048]{2,0,1:T(8,128)(2,1)} async-done(((bf16[14,32,2048]{2,0,1:T(8,128)(2,1)}), bf16[14,32,2048]{2,0,1:T(8,128)(2,1)}, u32[]{:S(2)}, u32[]{:S(2)}) %all-to-all-start.2) | async-done | bytes 1835040 | tf_op jit(solution)/shard_map/all_to_all | solution.py:42
  321.6 5.2 %all-to-all-start.1 = ((bf16[14,32,2048]{2,0,1:T(8,128)(2,1)}), bf16[14,32,2048]{2,0,1:T(8,128)(2,1)}, u32[]{:S(2)}, u32[]{:S(2)}) async-start(bf16[14,32,2048]{2,0,1:T(8,128)(2,1)} %copy.38), calls=%async_computation.1 | async-start | bytes 4194304 | tf_op jit(solution)/shard_map/all_to_all | solution.py:42
  326.8 2.6 multiply_convert_fusion
  329.4 2.4 copy.46
  331.7 23.5 %all-to-all-done.1 = bf16[14,32,2048]{2,0,1:T(8,128)(2,1)} async-done(((bf16[14,32,2048]{2,0,1:T(8,128)(2,1)}), bf16[14,32,2048]{2,0,1:T(8,128)(2,1)}, u32[]{:S(2)}, u32[]{:S(2)}) %all-to-all-start.1) | async-done | bytes 1835040 | tf_op jit(solution)/shard_map/all_to_all | solution.py:42
  355.3 4.5 %all-to-all-start.3 = ((bf16[14,32,2048]{2,0,1:T(8,128)(2,1)}), bf16[14,32,2048]{2,0,1:T(8,128)(2,1)S(1)}, u32[]{:S(2)}, u32[]{:S(2)}) async-start(bf16[14,32,2048]{2,0,1:T(8,128)(2,1)} %copy.46), calls=%async_computation.3 | async-start | bytes 4194304 | tf_op jit(solution)/shard_map/all_to_all | solution.py:42
  359.8 0.1 fusion.20
  359.9 0.2 copy.75
  360.1 0.7 copy-done
  360.9 0.8 copy.78
  361.7 0.1 select_reduce_fusion
  361.8 0.2 copy.76
  362.1 0.8 copy.79
  362.9 0.2 copy.74
  363.2 0.8 copy.77
  364.0 24.2 %all-to-all-done.3 = bf16[14,32,2048]{2,0,1:T(8,128)(2,1)S(1)} async-done(((bf16[14,32,2048]{2,0,1:T(8,128)(2,1)}), bf16[14,32,2048]{2,0,1:T(8,128)(2,1)S(1)}, u32[]{:S(2)}, u32[]{:S(2)}) %all-to-all-start.3) | async-done | bytes 1835040 | tf_op jit(solution)/shard_map/all_to_all | solution.py:42
  388.2 3.7 convolution_divide_fusion.1
  391.9 2.2 fusion.6
  394.1 4.1 %fusion.4 = (f32[3,1,14,2048]{3,0,2,1:T(4,128)S(1)}, bf16[3,1,14,2048]{3,0,2,1:T(4,128)(2,1)S(1)}, bf16[3,1,14,2048]{3,0,2,1:T(4,128)(2,1)S(1)}, f32[3,1,14,2048]{3,0,2,1:T(4,128)S(1)}) fusion(f32[3,14,2048]{2,0,1:T(4,128)S(1)} %bitcast.69, bf16[3,14,2048]{2,0,1:T(4,128)(2,1)S(1)} %bitcast.72, f32[3,14,2048]{2,0,1:T(4,128)S(1)} %convolution_divide_fusion.1, ...), kind=kOutput, calls=%fused_computation.31 | convolution fusion | flops 6967296 | bytes 4243660 | tf_op jit(solution)/shard_map/dot_general | solution.py:79
  398.3 0.6 pad_maximum_fusion
  398.9 1.6 copy.51
  400.5 0.6 pad_maximum_fusion.1
  401.1 1.2 copy.50
  (44 shorter events, 0.2 us)
Async XLA Ops:
  12.5 11.5 %copy-start.9 = (bf16[24,2048]{1,0:T(8,128)(2,1)S(1)}, bf16[24,2048]{1,0:T(8,128)(2,1)}, u32[]{:S(2)}) copy-start(bf16[24,2048]{1,0:T(8,128)(2,1)} %param.6) | copy-start | bytes 294916
  12.5 88.8 %all-to-all-start = ((bf16[3,14,32,2048]{3,1,0,2:T(8,128)(2,1)}), bf16[3,14,32,2048]{3,1,0,2:T(8,128)(2,1)}, u32[]{:S(2)}, u32[]{:S(2)}) async-start(bf16[3,14,32,2048]{3,1,0,2:T(8,128)(2,1)} %bitcast.60), calls=%async_computation | async-start | bytes 12582912 | tf_op jit(solution)/shard_map/all_to_all | solution.py:19
  23.9 86.9 %all-gather.2.cloned.1.call-start = ((), (), s32[]{:S(2)}) async-start(), calls=%async_computation.4 | async-start | bytes 1671168 | tf_op jit(solution)/shard_map/all_gather | solution.py:26
  24.9 244.5 %all-reduce.2.cloned.1.call-start = ((), (), s32[]{:S(2)}) async-start(), calls=%async_computation.5 | async-start | bytes 6291456 | tf_op jit(solution)/shard_map/psum | solution.py:37
  110.8 3.3 copy-start.5
  110.8 3.3 copy-start.15
  114.1 2.0 copy-start.18
  116.1 0.7 copy-start.3
  119.6 149.9 %copy-start.2 = (bf16[384,2048]{1,0:T(8,128)(2,1)S(1)}, bf16[384,2048]{1,0:T(8,128)(2,1)}, u32[]{:S(2)}) copy-start(bf16[384,2048]{1,0:T(8,128)(2,1)} %param.7) | copy-start | bytes 4718596
  269.4 3.2 copy-start.16
  269.4 3.2 copy-start.19
  272.6 1.2 copy-start.7
  276.1 17.1 %copy-start.8 = (f32[384,448]{0,1:T(8,128)S(1)}, f32[384,448]{0,1:T(8,128)}, u32[]{:S(2)}) copy-start(f32[384,448]{0,1:T(8,128)} %copy-done.7) | copy-start | bytes 2064388
  276.1 17.1 %copy-start.17 = (bf16[384,2048]{1,0:T(8,128)(2,1)S(1)}, bf16[384,2048]{1,0:T(8,128)(2,1)}, u32[]{:S(2)}) copy-start(bf16[384,2048]{1,0:T(8,128)(2,1)} %all-gather.2.cloned.1.call-done) | copy-start | bytes 4718596
  276.2 17.1 %copy-start.20 = (f32[384,448]{0,1:T(8,128)S(1)}, f32[384,448]{0,1:T(8,128)}, u32[]{:S(2)}) copy-start(f32[384,448]{0,1:T(8,128)} %copy-done.18) | copy-start | bytes 2064388
  276.2 45.5 %all-to-all-start.2 = ((bf16[14,32,2048]{2,0,1:T(8,128)(2,1)}), bf16[14,32,2048]{2,0,1:T(8,128)(2,1)}, u32[]{:S(2)}, u32[]{:S(2)}) async-start(bf16[14,32,2048]{2,0,1:T(8,128)(2,1)} %copy.42), calls=%async_computation.2 | async-start | bytes 4194304 | tf_op jit(solution)/shard_map/all_to_all | solution.py:42
  298.0 28.7 %copy-start.1 = (f32[384,2048]{1,0:T(8,128)S(1)}, f32[384,2048]{1,0:T(8,128)}, u32[]{:S(2)}) copy-start(f32[384,2048]{1,0:T(8,128)} %all-reduce.2.cloned.1.call-done) | copy-start | bytes 9437188
  298.0 28.7 %copy-start.4 = (bf16[384,448]{0,1:T(8,128)(2,1)S(1)}, bf16[384,448]{0,1:T(8,128)(2,1)}, u32[]{:S(2)}) copy-start(bf16[384,448]{0,1:T(8,128)(2,1)} %copy-done.3) | copy-start | bytes 1032196
  321.6 33.6 %all-to-all-start.1 = ((bf16[14,32,2048]{2,0,1:T(8,128)(2,1)}), bf16[14,32,2048]{2,0,1:T(8,128)(2,1)}, u32[]{:S(2)}, u32[]{:S(2)}) async-start(bf16[14,32,2048]{2,0,1:T(8,128)(2,1)} %copy.38), calls=%async_computation.1 | async-start | bytes 4194304 | tf_op jit(solution)/shard_map/all_to_all | solution.py:42
  331.7 28.0 %copy-start.6 = (f32[3,3,14,2048]{3,2,1,0:T(8,128)S(1)}, f32[3,3,14,2048]{3,2,1,0:T(8,128)}, u32[]{:S(2)}) copy-start(f32[3,3,14,2048]{3,2,1,0:T(8,128)} %param.9) | copy-start | bytes 3096580
  355.3 32.9 %all-to-all-start.3 = ((bf16[14,32,2048]{2,0,1:T(8,128)(2,1)}), bf16[14,32,2048]{2,0,1:T(8,128)(2,1)S(1)}, u32[]{:S(2)}, u32[]{:S(2)}) async-start(bf16[14,32,2048]{2,0,1:T(8,128)(2,1)} %copy.46), calls=%async_computation.3 | async-start | bytes 4194304 | tf_op jit(solution)/shard_map/all_to_all | solution.py:42
  359.8 1.1 copy-start
  359.8 1.9 copy-start.13
  359.8 1.9 copy-start.14
  388.2 3.7 copy-start.12
  391.9 2.3 copy-start.10
  391.9 2.3 copy-start.11
Sparse Core Ops, SparseCore 0:
  27.4 64.8 all-gather.1
  119.7 149.6 all-reduce.1
where the time goes:
time: 410 us; the launch traced here: 409 us
  waiting for transfers between devices  297 us (72%)
  starting transfers between devices  38.2 us (9%)
  local copies, waits for them, and re-layouts  29 us (7%)
  matrix products  27.3 us (7%)
  between operations  14.4 us (4%)
    psum x1, waiting for transfers between devices, per_device(): output = lax.psum(partial_out, 'tensor')  150 us
    all_to_all x1, waiting for transfers between devices, per_device(): lax.all_to_all(picked, 'path', split_axis=2, concat_axis=2, tiled=True)  76.3 us
    all_to_all x3, waiting for transfers between devices, send_back(): lax.all_to_all(delta.reshape(piece_shape), 'path', split_axis=1, concat_a...  71.2 us
    all_to_all x3, starting transfers between devices, send_back(): lax.all_to_all(delta.reshape(piece_shape), 'path', split_axis=1, concat_a...  26.7 us
    all_to_all x1, starting transfers between devices, per_device(): lax.all_to_all(picked, 'path', split_axis=2, concat_axis=2, tiled=True)  11.5 us
    dot_general x3, matrix products, per_device(): lax.dot_general(weighting_j, got, (((0,), (1,)), ((), ())), preferred_ele...  10.1 us
    slice x4, local copies, waits for them, and re-layouts, per_device(): gate_rows, up_rows, down_rows = (rows[0], rows[1], rows[2])  9.49 us
  transfers between devices with their start and end apart: 6, of which 5 were waited for; matrix products, arithmetic and copies ran while one was open for 6% of the time, Pallas kernels for 0%

commit v1 on v0

--- a/solution.py
+++ b/solution.py
@@ -34,7 +34,9 @@
     activated = gate_pre * sigmoid_gate
     hidden = (activated * up_proj).astype(jnp.bfloat16)
     partial_out = jnp.dot(hidden, down_rows, preferred_element_type=jnp.float32) / math.sqrt(FW)
-    output = lax.psum(partial_out, "tensor")
+    output = partial_out
+    for hop in (1, 2, 4, 8):
+        output = output + lax.ppermute(output, "tensor", [(dev, dev ^ hop) for dev in range(16)])
     cotangent = (4.0 * (output - teacher.astype(jnp.float32))).astype(jnp.bfloat16)
     piece_shape = (block_rows, path_count, width)
 

time: 410 us -> 1100 us (2.68)
  waiting for transfers between devices: 297 us -> 821 us
  starting transfers between devices: 38.2 us -> 201 us
    ppermute x0 -> x4, waiting for transfers between devices: none -> 674 us  [per_device(): lax.ppermute(output, 'tensor', [(dev, dev ^ hop) for dev in range(16)])]
    psum x1 -> x0, waiting for transfers between devices: 150 us -> none  [per_device(): output = lax.psum(partial_out, 'tensor')]
    all_to_all x3, starting transfers between devices: 26.7 us -> 169 us  [send_back(): lax.all_to_all(delta.reshape(piece_shape), 'path', split_axis=1, concat_a...]
    ppermute x0 -> x4, starting transfers between devices: none -> 20.6 us  [per_device(): lax.ppermute(output, 'tensor', [(dev, dev ^ hop) for dev in range(16)])]
  transfers between devices with their start and end apart: 6 -> 9, of which waited for: 5 -> 8; matrix products, arithmetic and copies ran while one was open for 6% -> 2% of each run, Pallas kernels for 0% -> 0%
where the time goes in v1:
time: 1100 us; the launch traced here: 1090 us
  waiting for transfers between devices  821 us (75%)
  starting transfers between devices  201 us (18%)
  local copies, waits for them, and re-layouts  28.1 us (3%)
  matrix products  24.2 us (2%)
  between operations  14.4 us (1%)
    ppermute x4, waiting for transfers between devices, per_device(): lax.ppermute(output, 'tensor', [(dev, dev ^ hop) for dev in range(16)])  674 us
    all_to_all x3, starting transfers between devices, send_back(): lax.all_to_all(delta.reshape(piece_shape), 'path', split_axis=1, concat_a...  169 us
    all_to_all x1, waiting for transfers between devices, per_device(): lax.all_to_all(picked, 'path', split_axis=2, concat_axis=2, tiled=True)  76.4 us
    all_to_all x3, waiting for transfers between devices, send_back(): lax.all_to_all(delta.reshape(piece_shape), 'path', split_axis=1, concat_a...  70.7 us
  transfers between devices with their start and end apart: 9, of which 8 were waited for; matrix products, arithmetic and copies ran while one was open for 2% of the time, Pallas kernels for 0%

profile of v1, /device:TPU:1, one launch (start us, length us, event | category | flops | bytes accessed | tf_op | source)
XLA Modules:
  0.0 1094.4 jit_solution(1403604534323607856)
XLA Ops:
  7.2 0.7 pad_clamp_fusion
  7.8 4.6 gather_fusion
  12.4 11.5 %all-to-all-start = ((bf16[3,14,32,2048]{3,1,0,2:T(8,128)(2,1)}), bf16[3,14,32,2048]{3,1,0,2:T(8,128)(2,1)}, u32[]{:S(2)}, u32[]{:S(2)}) async-start(bf16[3,14,32,2048]{3,1,0,2:T(8,128)(2,1)} %bitcast.62), calls=%async_computation | async-start | bytes 12582912 | tf_op jit(solution)/shard_map/all_to_all | solution.py:19
  24.1 0.7 fusion.12
  24.9 76.4 %all-to-all-done = bf16[3,14,32,2048]{3,1,0,2:T(8,128)(2,1)} async-done(((bf16[3,14,32,2048]{3,1,0,2:T(8,128)(2,1)}), bf16[3,14,32,2048]{3,1,0,2:T(8,128)(2,1)}, u32[]{:S(2)}, u32[]{:S(2)}) %all-to-all-start) | async-done | bytes 5505056 | tf_op jit(solution)/shard_map/all_to_all | solution.py:19
  101.3 4.0 fusion.19
  105.3 2.3 copy.35
  107.5 2.2 copy.36
  109.7 1.0 copy.37
  110.8 3.3 convolution_multiply_fusion.3
  114.1 2.0 multiply_convert_fusion.6
  116.1 1.0 convolution_multiply_fusion
  117.1 1.9 collective-permute-start
  119.0 66.7 %collective-permute-done = f32[384,2048]{1,0:T(8,128)S(1)} collective-permute-done((f32[384,2048]{1,0:T(8,128)S(1)}, f32[384,2048]{1,0:T(8,128)S(1)}, u32[]{:S(2)}, u32[]{:S(2)}) %collective-permute-start) | collective-permute-done | bytes 3145760 | tf_op jit(solution)/shard_map/ppermute | solution.py:39
  185.7 0.7 add.46
  186.4 1.9 collective-permute-start.1
  188.3 138.3 %collective-permute-done.1 = f32[384,2048]{1,0:T(8,128)S(1)} collective-permute-done((f32[384,2048]{1,0:T(8,128)S(1)}, f32[384,2048]{1,0:T(8,128)S(1)}, u32[]{:S(2)}, u32[]{:S(2)}) %collective-permute-start.1) | collective-permute-done | bytes 3145760 | tf_op jit(solution)/shard_map/ppermute | solution.py:39
  326.6 0.6 add.47
  327.2 5.5 collective-permute-start.2
  332.7 339.7 %collective-permute-done.2 = f32[384,2048]{1,0:T(8,128)S(1)} collective-permute-done((f32[384,2048]{1,0:T(8,128)S(1)}, f32[384,2048]{1,0:T(8,128)S(1)}, u32[]{:S(2)}, u32[]{:S(2)}) %collective-permute-start.2) | collective-permute-done | bytes 3145760 | tf_op jit(solution)/shard_map/ppermute | solution.py:39
  672.4 0.6 add.48
  673.0 11.3 %collective-permute-start.3 = (f32[384,2048]{1,0:T(8,128)S(1)}, f32[384,2048]{1,0:T(8,128)S(1)}, u32[]{:S(2)}, u32[]{:S(2)}) collective-permute-start(f32[384,2048]{1,0:T(8,128)S(1)} %add.48), channel_id=1, source_target_pairs={{0,8},{1,9},{2,10},{3,11},{4,12},{5,13},{6,14},{7,15},{8,0},{9,1},... | collective-permute-start | bytes 9437192 | tf_op jit(solution)/shard_map/ppermute | solution.py:39
  684.2 129.2 %collective-permute-done.3 = f32[384,2048]{1,0:T(8,128)S(1)} collective-permute-done((f32[384,2048]{1,0:T(8,128)S(1)}, f32[384,2048]{1,0:T(8,128)S(1)}, u32[]{:S(2)}, u32[]{:S(2)}) %collective-permute-start.3) | collective-permute-done | bytes 3145760 | tf_op jit(solution)/shard_map/ppermute | solution.py:39
  813.4 0.9 multiply_convert_fusion.3
  814.3 1.1 convolution_multiply_fusion.1
  815.5 1.1 multiply_convert_fusion.1
  816.7 2.4 copy.42
  819.0 158.8 %all-to-all-start.2 = ((bf16[14,32,2048]{2,0,1:T(8,128)(2,1)}), bf16[14,32,2048]{2,0,1:T(8,128)(2,1)S(1)}, u32[]{:S(2)}, u32[]{:S(2)}) async-start(bf16[14,32,2048]{2,0,1:T(8,128)(2,1)} %copy.42), calls=%async_computation.2 | async-start | bytes 4194304 | tf_op jit(solution)/shard_map/all_to_all | solution.py:44
  977.8 3.1 multiply_convert_fusion.2
  980.9 2.3 copy.38
  983.2 22.9 %all-to-all-done.2 = bf16[14,32,2048]{2,0,1:T(8,128)(2,1)S(1)} async-done(((bf16[14,32,2048]{2,0,1:T(8,128)(2,1)}), bf16[14,32,2048]{2,0,1:T(8,128)(2,1)S(1)}, u32[]{:S(2)}, u32[]{:S(2)}) %all-to-all-start.2) | async-done | bytes 1835040 | tf_op jit(solution)/shard_map/all_to_all | solution.py:44
  1006.2 5.2 all-to-all-start.1
  1011.3 2.5 multiply_convert_fusion
  1013.9 2.4 copy.46
  1016.2 23.6 %all-to-all-done.1 = bf16[14,32,2048]{2,0,1:T(8,128)(2,1)} async-done(((bf16[14,32,2048]{2,0,1:T(8,128)(2,1)}), bf16[14,32,2048]{2,0,1:T(8,128)(2,1)}, u32[]{:S(2)}, u32[]{:S(2)}) %all-to-all-start.1) | async-done | bytes 1835040 | tf_op jit(solution)/shard_map/all_to_all | solution.py:44
  1039.8 5.2 all-to-all-start.3
  1045.4 0.7 copy-done
  1046.1 0.8 copy.78
  1047.3 0.8 copy.79
  1048.4 0.8 copy.77
  1049.2 24.2 %all-to-all-done.3 = bf16[14,32,2048]{2,0,1:T(8,128)(2,1)} async-done(((bf16[14,32,2048]{2,0,1:T(8,128)(2,1)}), bf16[14,32,2048]{2,0,1:T(8,128)(2,1)}, u32[]{:S(2)}, u32[]{:S(2)}) %all-to-all-start.3) | async-done | bytes 1835040 | tf_op jit(solution)/shard_map/all_to_all | solution.py:44
  1073.5 2.1 convolution_divide_fusion.1
  1075.5 3.9 fusion.6
  1079.4 4.1 fusion.4
  1083.6 0.6 pad_maximum_fusion
  1084.2 1.6 copy.51
  1085.8 0.6 pad_maximum_fusion.1
  1086.4 1.2 copy.50
  (37 shorter events, 1.2 us)
Async XLA Ops:
  12.4 11.5 %copy-start.5 = (bf16[24,2048]{1,0:T(8,128)(2,1)S(1)}, bf16[24,2048]{1,0:T(8,128)(2,1)}, u32[]{:S(2)}) copy-start(bf16[24,2048]{1,0:T(8,128)(2,1)} %param.6) | copy-start | bytes 294916
  12.4 88.8 %all-to-all-start = ((bf16[3,14,32,2048]{3,1,0,2:T(8,128)(2,1)}), bf16[3,14,32,2048]{3,1,0,2:T(8,128)(2,1)}, u32[]{:S(2)}, u32[]{:S(2)}) async-start(bf16[3,14,32,2048]{3,1,0,2:T(8,128)(2,1)} %bitcast.62), calls=%async_computation | async-start | bytes 12582912 | tf_op jit(solution)/shard_map/all_to_all | solution.py:19
  23.9 86.9 %all-gather.2.cloned.1.call-start = ((), (), s32[]{:S(2)}) async-start(), calls=%async_computation.4 | async-start | bytes 1671168 | tf_op jit(solution)/shard_map/all_gather | solution.py:26
  110.8 3.3 copy-start.1
  110.8 3.3 copy-start.11
  117.1 68.6 %collective-permute-start = (f32[384,2048]{1,0:T(8,128)S(1)}, f32[384,2048]{1,0:T(8,128)S(1)}, u32[]{:S(2)}, u32[]{:S(2)}) collective-permute-start(f32[384,2048]{1,0:T(8,128)S(1)} %convolution_multiply_fusion), channel_id=1, source_target_pairs={{0,1},{1,0},{2,3},{3,2},{4,5},{5,4},{6,7},{7,6},{8,9},{9,8},{10,11... | collective-permute-start | bytes 9437192 | tf_op jit(solution)/shard_map/ppermute | solution.py:39
  186.4 140.2 %collective-permute-start.1 = (f32[384,2048]{1,0:T(8,128)S(1)}, f32[384,2048]{1,0:T(8,128)S(1)}, u32[]{:S(2)}, u32[]{:S(2)}) collective-permute-start(f32[384,2048]{1,0:T(8,128)S(1)} %add.46), channel_id=1, source_target_pairs={{0,2},{1,3},{2,0},{3,1},{4,6},{5,7},{6,4},{7,5},{8,10},{9,11},{10,... | collective-permute-start | bytes 9437192 | tf_op jit(solution)/shard_map/ppermute | solution.py:39
  327.2 486.3 %copy-start.2 = (bf16[384,2048]{1,0:T(8,128)(2,1)S(1)}, bf16[384,2048]{1,0:T(8,128)(2,1)}, u32[]{:S(2)}) copy-start(bf16[384,2048]{1,0:T(8,128)(2,1)} %param.7) | copy-start | bytes 4718596
  327.2 345.2 %collective-permute-start.2 = (f32[384,2048]{1,0:T(8,128)S(1)}, f32[384,2048]{1,0:T(8,128)S(1)}, u32[]{:S(2)}, u32[]{:S(2)}) collective-permute-start(f32[384,2048]{1,0:T(8,128)S(1)} %add.47), channel_id=1, source_target_pairs={{0,4},{1,5},{2,6},{3,7},{4,0},{5,1},{6,2},{7,3},{8,12},{9,13},{10,... | collective-permute-start | bytes 9437192 | tf_op jit(solution)/shard_map/ppermute | solution.py:39
  673.0 140.5 %collective-permute-start.3 = (f32[384,2048]{1,0:T(8,128)S(1)}, f32[384,2048]{1,0:T(8,128)S(1)}, u32[]{:S(2)}, u32[]{:S(2)}) collective-permute-start(f32[384,2048]{1,0:T(8,128)S(1)} %add.48), channel_id=1, source_target_pairs={{0,8},{1,9},{2,10},{3,11},{4,12},{5,13},{6,14},{7,15},{8,0},{9,1},... | collective-permute-start | bytes 9437192 | tf_op jit(solution)/shard_map/ppermute | solution.py:39
  814.3 1.2 copy-start.3
  815.5 1.2 copy-start.12
  819.0 187.1 %all-to-all-start.2 = ((bf16[14,32,2048]{2,0,1:T(8,128)(2,1)}), bf16[14,32,2048]{2,0,1:T(8,128)(2,1)S(1)}, u32[]{:S(2)}, u32[]{:S(2)}) async-start(bf16[14,32,2048]{2,0,1:T(8,128)(2,1)} %copy.42), calls=%async_computation.2 | async-start | bytes 4194304 | tf_op jit(solution)/shard_map/all_to_all | solution.py:44
  1006.2 33.6 %all-to-all-start.1 = ((bf16[14,32,2048]{2,0,1:T(8,128)(2,1)}), bf16[14,32,2048]{2,0,1:T(8,128)(2,1)}, u32[]{:S(2)}, u32[]{:S(2)}) async-start(bf16[14,32,2048]{2,0,1:T(8,128)(2,1)} %copy.38), calls=%async_computation.1 | async-start | bytes 4194304 | tf_op jit(solution)/shard_map/all_to_all | solution.py:44
  1016.2 28.8 %copy-start.4 = (f32[3,3,14,2048]{3,2,1,0:T(8,128)S(1)}, f32[3,3,14,2048]{3,2,1,0:T(8,128)}, u32[]{:S(2)}) copy-start(f32[3,3,14,2048]{3,2,1,0:T(8,128)} %param.9) | copy-start | bytes 3096580
  1039.8 33.7 %all-to-all-start.3 = ((bf16[14,32,2048]{2,0,1:T(8,128)(2,1)}), bf16[14,32,2048]{2,0,1:T(8,128)(2,1)}, u32[]{:S(2)}, u32[]{:S(2)}) async-start(bf16[14,32,2048]{2,0,1:T(8,128)(2,1)} %copy.46), calls=%async_computation.3 | async-start | bytes 4194304 | tf_op jit(solution)/shard_map/all_to_all | solution.py:44
  1045.0 1.1 copy-start
  1045.0 1.9 copy-start.9
  1045.0 1.9 copy-start.10
  1073.5 2.1 copy-start.8
  1075.5 3.9 copy-start.6
  1075.5 3.9 copy-start.7
Sparse Core Ops, SparseCore 0:
  27.4 64.7 all-gather.1
